TPU v7x, 256 devices: a whole 4x4x8 slice. The times are simulated.
256 devices in a mesh: blk: 64 (over y, x_lo, z), team: 4 (over x_hi, core).
Axes of the slice: x: 4 (x_hi: 2, x_lo: 2; x = x_hi * 2 + x_lo), y: 4, z: 8, core: 2. Of those that a mesh axis runs over, the one named last changes fastest.
Arguments:
- loadings: bfloat16 [64, 98304], P(None, ('blk', 'team')), may hold values from -6 to 6
- scales: bfloat16 [64, 768], P(None, ('blk', 'team')), may hold values from 0.25 to 4
- cov: bfloat16 [16384, 16, 4, 1536], P('blk', None, 'team'), may hold values from -0.01953125 to 0.01953125
Outputs:
- product: float32 [64, 16384], P(None, 'blk')
All inputs are finite; a program needn't handle non-finite values.
Results may differ from a plain program's by a relative error of at most 0.0028.
Values may be sent and summed in bfloat16 or wider, within the bound.
No kernel may reach another device: no remote copies, remote signals or barrier semaphores. Data moves between devices by JAX's collectives and lax.ppermute only.
A program may use at most 128 MiB of HBM per device.

v0:
```python
import jax
import jax.numpy as jnp
from jax import lax
from jax.sharding import PartitionSpec as P


def per_device(loadings, scales, cov):
    n_loads, width = loadings.shape
    groups = scales.shape[1]
    team_size = lax.axis_size("team")
    blk_size = lax.axis_size("blk")
    scaled = (
        (
            loadings.astype(jnp.float32).reshape(n_loads, groups, width // groups)
            * scales.astype(jnp.float32)[:, :, None]
        )
        .reshape(n_loads, width)
        .astype(jnp.bfloat16)
    )
    pairs = []
    for b in range(blk_size):
        c, d = divmod(b, team_size)
        for p in range(team_size):
            pairs.append((b * team_size + p, (c * team_size + p) * team_size + d))
    moved = lax.ppermute(scaled, ("blk", "team"), pairs)
    gathered = lax.all_gather(moved, "blk", axis=1, tiled=True)
    stops = cov.shape[1]
    gathered = gathered.reshape(n_loads, stops, cov.shape[3])
    cov_local = cov[:, :, 0, :]
    part = lax.dot_general(
        gathered, cov_local, (((1, 2), (1, 2)), ((), ())), preferred_element_type=jnp.float32
    )
    return lax.psum(part, "team")


def solution(mesh):
    placed = (P(None, ("blk", "team")), P(None, ("blk", "team")), P("blk", None, "team", None))
    return jax.shard_map(
        per_device, mesh=mesh, in_specs=placed, out_specs=P(None, "blk"), check_vma=False
    )
```

profile of v0, /device:TPU:1, one launch (start us, length us, event | category | flops | bytes accessed | tf_op | source)
XLA Modules:
  0.0 395.1 jit_solution(3153705874606790821)
XLA Ops:
  6.5 0.0 all-gather.2.cloned.1.call-start
  6.5 0.8 copy.6
  7.3 0.1 mul.11
  7.4 0.8 fusion.9
  8.3 4.9 %collective-permute-start = (bf16[64,384]{1,0:T(8,128)(2,1)S(1)}, bf16[64,384]{1,0:T(8,128)(2,1)S(1)}, u32[]{:S(2)}, u32[]{:S(2)}) collective-permute-start(bf16[64,384]{1,0:T(8,128)(2,1)S(1)} %fusion.9), channel_id=1, source_target_pairs={{0,0},{1,4},{2,8},{3,12},{4,1},{5,5},{6,9},{7,13},{8,2},{9,6},{10,... | collective-permute-start | bytes 147464 | tf_op jit(solution)/shard_map/ppermute | solution.py:25
  13.2 1.8 collective-permute-done
  15.0 0.0 copy-start
  15.0 0.6 copy-done
  15.6 0.0 all-gather.2.cloned.1.call-update
  15.6 0.0 all-reduce.2.cloned.1.call-start
  15.7 265.7 %all-gather.2.cloned.1.call-done = bf16[64,24576]{1,0:T(8,128)(2,1)} async-done(((bf16[64,384]{1,0:T(8,128)(2,1)}), bf16[64,24576]{1,0:T(8,128)(2,1)}) %all-gather.2.cloned.1.call-update) | async-done | bytes 3145744 | tf_op jit(solution)/shard_map/all_gather | solution.py:26
  281.4 19.6 %fusion.4 = f32[64,256]{1,0:T(8,128)} fusion(bf16[256,16,1536]{2,1,0:T(8,128)(2,1)} %bitcast.15, bf16[8,16,8,1536]{3,2,1,0:T(8,128)(2,1)} %bitcast.16), kind=kOutput, calls=%fused_computation.4 | convolution fusion | flops 805306368 | bytes 15794176 | tf_op jit(solution)/shard_map/dot_general | solution.py:30
  301.0 0.0 all-reduce.2.cloned.1.call-update
  301.1 85.7 %all-reduce.2.cloned.1.call-done = f32[64,256]{1,0:T(8,128)} async-done(((f32[64,256]{1,0:T(8,128)}), f32[64,256]{1,0:T(8,128)}) %all-reduce.2.cloned.1.call-update) | async-done | bytes 65552 | tf_op jit(solution)/shard_map/psum | solution.py:33
  386.7 1.5 copy.23
Async XLA Ops:
  6.5 274.9 %all-gather.2.cloned.1.call-start = ((), (), s32[]{:S(2)}) async-start(), calls=%async_computation | async-start | bytes 3194880 | tf_op jit(solution)/shard_map/all_gather | solution.py:26
  8.3 6.7 %collective-permute-start = (bf16[64,384]{1,0:T(8,128)(2,1)S(1)}, bf16[64,384]{1,0:T(8,128)(2,1)S(1)}, u32[]{:S(2)}, u32[]{:S(2)}) collective-permute-start(bf16[64,384]{1,0:T(8,128)(2,1)S(1)} %fusion.9), channel_id=1, source_target_pairs={{0,0},{1,4},{2,8},{3,12},{4,1},{5,5},{6,9},{7,13},{8,2},{9,6},{10,... | collective-permute-start | bytes 147464 | tf_op jit(solution)/shard_map/ppermute | solution.py:25
  15.0 0.6 copy-start
  15.6 371.1 %all-reduce.2.cloned.1.call-start = ((), (), s32[]{:S(2)}) async-start(), calls=%async_computation.1 | async-start | bytes 131072 | tf_op jit(solution)/shard_map/psum | solution.py:33
Sparse Core Ops, SparseCore 0:
  15.7 265.6 all-gather.1
  301.2 85.5 all-reduce.1
where the time goes:
time: 395 us
  waiting for transfers between devices  353 us (89%)
  matrix products  19.6 us (5%)
  between operations  13.4 us (3%)
  starting transfers between devices  4.98 us (1%)
    all_gather x1, waiting for transfers between devices, per_device(): gathered = lax.all_gather(moved, 'blk', axis=1, tiled=True)  266 us
    psum x1, waiting for transfers between devices, per_device(): return lax.psum(part, 'team')  85.7 us
    dot_general x1, matrix products, per_device(): lax.dot_general(gathered, cov_local, (((1, 2), (1, 2)), ((), ())), prefer...  19.6 us
  transfers between devices with their start and end apart: 3, of which 3 were waited for; matrix products, arithmetic and copies ran while one was open for 0% of the time, Pallas kernels for 0%

commit v1 on v0

--- a/solution.py
+++ b/solution.py
@@ -23,7 +23,9 @@
         for p in range(team_size):
             pairs.append((b * team_size + p, (c * team_size + p) * team_size + d))
     moved = lax.ppermute(scaled, ("blk", "team"), pairs)
-    gathered = lax.all_gather(moved, "blk", axis=1, tiled=True)
+    gathered = jnp.concatenate(
+        lax.all_to_all(jnp.stack([moved] * lax.axis_size("blk")), "blk", 0, 0), axis=1
+    )
     stops = cov.shape[1]
     gathered = gathered.reshape(n_loads, stops, cov.shape[3])
     cov_local = cov[:, :, 0, :]

time: 395 us -> 184 us (0.47)
  waiting for transfers between devices: 353 us -> 51.2 us
  blocking collectives: 0 us -> 83.2 us
  local copies, waits for them, and re-layouts: 2.99 us -> 7.92 us
    all_gather x1 -> x0, waiting for transfers between devices: 266 us -> none  [per_device(): gathered = lax.all_gather(moved, 'blk', axis=1, tiled=True)]
    all_to_all x0 -> x1, blocking collectives: none -> 83.2 us  [per_device(): lax.all_to_all(jnp.stack([moved] * lax.axis_size('blk')), 'blk', 0, 0)]
    psum x1, waiting for transfers between devices: 85.7 us -> 49.4 us  [per_device(): return lax.psum(part, 'team')]
  transfers between devices with their start and end apart: 3 -> 2, of which waited for: 3 -> 2; matrix products, arithmetic and copies ran while one was open for 0% -> 0% of each run, Pallas kernels for 0% -> 0%
where the time goes in v1:
time: 184 us
  blocking collectives  83.2 us (45%)
  waiting for transfers between devices  51.2 us (28%)
  matrix products  22.7 us (12%)
  between operations  13.4 us (7%)
  local copies, waits for them, and re-layouts  7.92 us (4%)
  starting transfers between devices  4.94 us (3%)
    all_to_all x1, blocking collectives, per_device(): lax.all_to_all(jnp.stack([moved] * lax.axis_size('blk')), 'blk', 0, 0)  83.2 us
    psum x1, waiting for transfers between devices, per_device(): return lax.psum(part, 'team')  49.4 us
    dot_general x1, matrix products, per_device(): lax.dot_general(gathered, cov_local, (((1, 2), (1, 2)), ((), ())), prefer...  22.7 us
    ppermute x1, starting transfers between devices, per_device(): moved = lax.ppermute(scaled, ('blk', 'team'), pairs)  4.94 us
  transfers between devices with their start and end apart: 2, of which 2 were waited for; matrix products, arithmetic and copies ran while one was open for 0% of the time, Pallas kernels for 0%

profile of v1, /device:TPU:1, one launch (start us, length us, event | category | flops | bytes accessed | tf_op | source)
XLA Modules:
  0.0 184.1 jit_solution(7296556760959173800)
XLA Ops:
  6.5 0.0 all-reduce.2.cloned.1.call-start
  6.5 0.8 copy.9
  7.3 0.1 mul.11
  7.4 0.8 fusion.8
  8.3 4.9 %collective-permute-start = (bf16[64,384]{1,0:T(8,128)(2,1)S(1)}, bf16[64,384]{1,0:T(8,128)(2,1)S(1)}, u32[]{:S(2)}, u32[]{:S(2)}) collective-permute-start(bf16[64,384]{1,0:T(8,128)(2,1)S(1)} %fusion.8), channel_id=1, source_target_pairs={{0,0},{1,4},{2,8},{3,12},{4,1},{5,5},{6,9},{7,13},{8,2},{9,6},{10,... | collective-permute-start | bytes 147464 | tf_op jit(solution)/shard_map/ppermute | solution.py:25
  13.2 1.8 collective-permute-done
  15.0 0.5 stack.2
  15.5 83.2 %all_to_all.5 = bf16[64,64,384]{2,1,0:T(8,128)(2,1)S(1)} all-to-all(bf16[64,64,384]{2,1,0:T(8,128)(2,1)S(1)} %stack.2), channel_id=1, replica_groups=mesh['blk'=64,'team'=4] {'blk'}, dimensions={0} | all-to-all | bytes 6291456 | tf_op jit(solution)/shard_map/all_to_all | solution.py:27
  98.7 1.9 %copy.10 = bf16[64,64,384]{2,1,0:T(8,128)(2,1)S(1)} copy(bf16[64,64,384]{2,0,1:T(8,128)(2,1)S(1)} %bitcast.9) | data formatting | bytes 6291456 | tf_op jit(solution)/shard_map/reshape | solution.py:26
  100.5 3.2 %reshape_reshape.3 = bf16[64,16,1536]{2,1,0:T(8,128)(2,1)} reshape(bf16[64,64,384]{2,1,0:T(8,128)(2,1)S(1)} %copy.10) | data formatting | bytes 6291456 | tf_op jit(solution)/shard_map/reshape;reshape | solution.py:30
  103.7 22.7 %fusion.3 = f32[64,256]{1,0:T(8,128)} fusion(bf16[256,16,1536]{2,1,0:T(8,128)(2,1)} %bitcast.11, bf16[64,16,1536]{2,1,0:T(8,128)(2,1)} %reshape_reshape.3), kind=kOutput, calls=%fused_computation.3 | convolution fusion | flops 805306368 | bytes 15794176 | tf_op jit(solution)/shard_map/dot_general | solution.py:32
  126.4 0.0 all-reduce.2.cloned.1.call-update
  126.4 49.4 %all-reduce.2.cloned.1.call-done = f32[64,256]{1,0:T(8,128)} async-done(((f32[64,256]{1,0:T(8,128)}), f32[64,256]{1,0:T(8,128)}) %all-reduce.2.cloned.1.call-update) | async-done | bytes 65552 | tf_op jit(solution)/shard_map/psum | solution.py:35
  175.8 1.5 copy.24
Async XLA Ops:
  6.5 169.3 %all-reduce.2.cloned.1.call-start = ((), (), s32[]{:S(2)}) async-start(), calls=%async_computation.1 | async-start | bytes 131072 | tf_op jit(solution)/shard_map/psum | solution.py:35
  8.3 6.7 %collective-permute-start = (bf16[64,384]{1,0:T(8,128)(2,1)S(1)}, bf16[64,384]{1,0:T(8,128)(2,1)S(1)}, u32[]{:S(2)}, u32[]{:S(2)}) collective-permute-start(bf16[64,384]{1,0:T(8,128)(2,1)S(1)} %fusion.8), channel_id=1, source_target_pairs={{0,0},{1,4},{2,8},{3,12},{4,1},{5,5},{6,9},{7,13},{8,2},{9,6},{10,... | collective-permute-start | bytes 147464 | tf_op jit(solution)/shard_map/ppermute | solution.py:25
Sparse Core Ops, SparseCore 0:
  126.5 49.2 all-reduce.1
